TPU v7x, 512 devices: a whole 4x4x16 slice. The times are simulated.
512 devices in a mesh: row: 32 (over x, y, core), col: 16 (over z).
Axes of the slice: x: 4, y: 4, z: 16, core: 2. Of those that a mesh axis runs over, the one named last changes fastest.
Arguments:
- panel: float32 [65536, 256], P('row', 'col'), may hold values from -210 to 210
- slab: float32 [65536, 4096], P('row', 'col'), may hold values from -6 to 6
Outputs:
- triangle: float32 [256, 256], P(None, 'col')
- projected: float32 [256, 4096], P(None, 'col')
- residual: float32 [65536, 4096], P('row', 'col')
All inputs are finite; a program needn't handle non-finite values.
Results may differ from a plain program's by a relative error of at most 0.0003.
Values sent between devices are 32-bit elements; how exact they have to be, the bound alone decides.
No kernel may reach another device: no remote copies, remote signals or barrier semaphores. Data moves between devices by JAX's collectives and lax.ppermute only.
A program may use at most 64 MiB of HBM per device.

v0:
```python
import math
import jax
import jax.numpy as jnp
from jax import lax
from jax.sharding import PartitionSpec as P

contract_rows = (((0,), (0,)), ((), ()))


def row_sum(x):
    n = lax.axis_size("row")
    rows, cols = x.shape
    parts = x.reshape(n, rows // n, cols)
    mine = lax.all_to_all(parts, "row", 0, 0, tiled=False).sum(0)
    copies = jnp.broadcast_to(mine[None], (n, rows // n, cols))
    return lax.all_to_all(copies, "row", 0, 0, tiled=False).reshape(rows, cols)


def per_device(panel, slab):
    highest = lax.Precision.HIGHEST
    gathered = lax.all_gather(panel, "col", axis=1, tiled=True)
    cross_local = lax.dot_general(gathered, slab, contract_rows, precision=highest)
    gram_local = lax.dot_general(gathered, gathered, contract_rows, precision=highest)
    width = gram_local.shape[1]
    summed = row_sum(jnp.concatenate([gram_local, cross_local], axis=1))
    gram_total, totals = (summed[:, :width], summed[:, width:])
    lower_factor = jnp.linalg.cholesky(gram_total)
    projected = lax.linalg.triangular_solve(
        lower_factor, totals, left_side=True, lower=True, transpose_a=False
    )
    coefficients = lax.linalg.triangular_solve(
        lower_factor, projected, left_side=True, lower=True, transpose_a=True
    )
    residual = slab - jnp.dot(gathered, coefficients, precision=highest)
    col_width = panel.shape[1]
    rows_total = gathered.shape[0] * lax.axis_size("row")
    scaled = lower_factor.T * (1.0 / math.sqrt(rows_total))
    triangle = lax.dynamic_slice_in_dim(scaled, lax.axis_index("col") * col_width, col_width, 1)
    return (triangle, projected, residual)


def solution(mesh):
    placed = (P("row", "col"), P("row", "col"))
    return jax.shard_map(
        per_device,
        mesh=mesh,
        in_specs=placed,
        out_specs=(P(None, "col"), P(None, "col"), P("row", "col")),
        check_vma=False,
    )
```

profile of v0, /device:TPU:1, one launch (start us, length us, event | category | flops | bytes accessed | tf_op | source)
XLA Modules:
  0.0 207.8 jit_solution(18180346574200016031)
XLA Ops:
  7.2 0.0 all-gather.2.cloned.1.call-start
  7.2 0.7 all-gather.2.cloned.1.call-update
  7.9 71.6 %all-gather.2.cloned.1.call-done = f32[2048,256]{0,1:T(8,128)} async-done(((f32[2048,16]{0,1:T(8,128)}), f32[2048,256]{0,1:T(8,128)}) %all-gather.2.cloned.1.call-update) | async-done | bytes 2097168 | tf_op jit(solution)/shard_map/all_gather | solution.py:21
  79.5 0.0 copy-start
  79.5 0.0 copy-start.2
  79.5 4.2 %fusion.19 = f32[256,256]{0,1:T(8,128)S(1)} fusion(f32[2048,256]{0,1:T(8,128)} %all-gather.2.cloned.1.call-done), kind=kOutput, calls=%fused_computation.43 | convolution fusion | flops 1610612736 | bytes 2359296 | tf_op jit(solution)/shard_map/dot_general | solution.py:23
  83.7 0.0 copy-done
  83.7 0.0 copy-done.2
  83.7 3.6 %fusion.20 = f32[256,256]{0,1:T(8,128)S(1)} fusion(f32[2048,256]{0,1:T(8,128)S(1)} %copy-done, f32[2048,256]{1,0:T(8,128)S(1)} %copy-done.2), kind=kOutput, calls=%fused_computation.44 | convolution fusion | flops 1610612736 | bytes 4456448 | tf_op jit(solution)/shard_map/dot_general | solution.py:22
  87.3 0.2 copy.8
  87.5 28.0 %all_to_all.10 = f32[32,8,512]{2,1,0:T(8,128)S(1)} all-to-all(f32[32,8,512]{2,1,0:T(8,128)S(1)} %bitcast.53), channel_id=1, replica_groups=mesh['row'=32,'col'=16] {'row'}, dimensions={0} | all-to-all | bytes 1048576 | tf_op jit(solution)/shard_map/all_to_all | solution.py:14
  115.6 0.8 broadcast_in_dim.3
  116.4 3.9 %all-to-all-start.1 = ((f32[32,8,512]{2,1,0:T(8,128)}), f32[32,8,512]{2,1,0:T(8,128)S(1)}, u32[]{:S(2)}, u32[]{:S(2)}) async-start(f32[32,8,512]{2,1,0:T(8,128)} %broadcast_in_dim.3), calls=%async_computation.1 | async-start | bytes 1048576 | tf_op jit(solution)/shard_map/all_to_all | solution.py:16
  120.3 2.9 %copy.11 = f32[2048,256]{0,1:T(8,128)} copy(f32[2048,256]{1,0:T(8,128)} %param.3) | data formatting | bytes 4194304 | tf_op args[1]
  123.2 8.5 %all-to-all-done.1 = f32[32,8,512]{2,1,0:T(8,128)S(1)} async-done(((f32[32,8,512]{2,1,0:T(8,128)}), f32[32,8,512]{2,1,0:T(8,128)S(1)}, u32[]{:S(2)}, u32[]{:S(2)}) %all-to-all-start.1) | async-done | bytes 524320 | tf_op jit(solution)/shard_map/all_to_all | solution.py:16
  131.7 0.1 copy.13
  131.9 11.7 %cholesky.50 = f32[128,128]{1,0:T(8,128)S(1)} custom-call(f32[128,128]{1,0:T(8,128)S(1)} %cholesky.118), custom_call_target="Cholesky" | custom-call | tf_op jit(solution)/shard_map/jit(cholesky)/cholesky | solution.py:27
  143.7 9.8 %custom-call.16 = f32[1,128,128]{1,2,0:T(8,128)S(1)} custom-call(f32[1,128,128]{2,1,0:T(8,128)S(1)} %get-tuple-element.32), custom_call_target="InvertDiagBlocksLowerTriangular" | custom-call | tf_op jit(solution)/shard_map/jit(cholesky)/cholesky | solution.py:27
  153.5 0.2 constant_dynamic-update-slice_fusion
  153.7 0.3 convolution_subtract_fusion.2
  154.0 11.7 %cholesky.105 = f32[128,128]{1,0:T(8,128)S(1)} custom-call(f32[128,128]{1,0:T(8,128)S(1)} %convolution_subtract_fusion.2), custom_call_target="Cholesky" | custom-call | tf_op jit(solution)/shard_map/jit(cholesky)/cholesky | solution.py:27
  165.7 0.6 compare_reduce_fusion
  167.7 0.1 triangular_solve.53
  167.8 4.0 %while.1 = (s32[]{:T(128)}, f32[256,256]{1,0:T(8,128)S(1)}, s32[2,2]{1,0:T(2,128)S(1)}, f32[2,128,128]{2,1,0:T(8,128)S(1)}, s32[]{:T(128)}) while((s32[]{:T(128)}, f32[256,256]{1,0:T(8,128)S(1)}, s32[2,2]{1,0:T(2,128)S(1)}, f32[2,128,128]{2,1,0:T(8,128)S(1)}, s32[]{:T(128)}) %tuple.30), condition=%wide.while_cond, body=%wide.while_body.sunk | while | flops 2 | bytes 131189 | solution.py:28
  167.8 0.6 fusion.34
  168.4 1.4 bitcast_dynamic-update-slice_fusion.2
  169.8 0.6 fusion.34
  170.4 1.4 bitcast_dynamic-update-slice_fusion.2
  171.8 19.9 %custom-call.17 = f32[2,128,128]{1,2,0:T(8,128)S(1)} custom-call(f32[2,128,128]{2,1,0:T(8,128)S(1)} %get-tuple-element.10), custom_call_target="InvertDiagBlocksLowerTriangular" | custom-call | tf_op jit(solution)/shard_map/triangular_solve | solution.py:28
  191.7 0.0 copy-start.1
  191.7 0.3 fusion.6
  192.0 0.3 convolution_subtract_fusion.1
  192.3 0.3 fusion.13
  192.6 0.3 fusion.12
  192.9 0.7 pad_maximum_fusion.1
  193.6 0.3 convolution_subtract_fusion
  193.9 0.3 fusion.11
  194.2 0.0 copy-done.1
  194.2 3.3 %fusion = f32[2048,256]{0,1:T(8,128)} fusion(f32[2048,256]{0,1:T(8,128)S(1)} %copy-done.1, f32[2048,256]{0,1:T(8,128)S(1)} %copy-done, f32[128,256]{1,0:T(8,128)S(1)} %fusion.12, f32[128,256]{1,0:T(8,128)S(1)} %fusion.11), kind=kOutput, calls=%fused_computation.3 | convolution fusion | flops 1611202560 | bytes 6553600 | tf_op jit(solution)/shard_map/dot_general | solution.py:34
  197.5 2.9 %copy.12 = f32[2048,256]{1,0:T(8,128)} copy(f32[2048,256]{0,1:T(8,128)} %fusion) | data formatting | bytes 4194304
  200.4 0.6 fusion.16
  (13 shorter events, 0.3 us)
Async XLA Ops:
  7.2 72.3 %all-gather.2.cloned.1.call-start = ((), (), s32[]{:S(2)}) async-start(), calls=%async_computation.2 | async-start | bytes 2228224 | tf_op jit(solution)/shard_map/all_gather | solution.py:21
  79.5 4.2 %copy-start = (f32[2048,256]{0,1:T(8,128)S(1)}, f32[2048,256]{0,1:T(8,128)}, u32[]{:S(2)}) copy-start(f32[2048,256]{0,1:T(8,128)} %all-gather.2.cloned.1.call-done) | copy-start | bytes 6291460
  79.5 4.2 %copy-start.2 = (f32[2048,256]{1,0:T(8,128)S(1)}, f32[2048,256]{1,0:T(8,128)}, u32[]{:S(2)}) copy-start(f32[2048,256]{1,0:T(8,128)} %param.3) | copy-start | bytes 6291460
  116.4 15.3 %all-to-all-start.1 = ((f32[32,8,512]{2,1,0:T(8,128)}), f32[32,8,512]{2,1,0:T(8,128)S(1)}, u32[]{:S(2)}, u32[]{:S(2)}) async-start(f32[32,8,512]{2,1,0:T(8,128)} %broadcast_in_dim.3), calls=%async_computation.1 | async-start | bytes 1048576 | tf_op jit(solution)/shard_map/all_to_all | solution.py:16
  191.7 2.5 %copy-start.1 = (f32[2048,256]{0,1:T(8,128)S(1)}, f32[2048,256]{0,1:T(8,128)}, u32[]{:S(2)}) copy-start(f32[2048,256]{0,1:T(8,128)} %copy.11) | copy-start | bytes 6291460
Sparse Core Ops, SparseCore 0:
  10.1 69.3 all-gather.1
where the time goes:
time: 208 us
  waiting for transfers between devices  80.7 us (39%)
  other arithmetic  55.3 us (27%)
  blocking collectives  28 us (13%)
  between operations  15.5 us (7%)
  matrix products  13.3 us (6%)
  local copies, waits for them, and re-layouts  11 us (5%)
  starting transfers between devices  3.89 us (2%)
    all_gather x1, waiting for transfers between devices, per_device(): gathered = lax.all_gather(panel, 'col', axis=1, tiled=True)  71.6 us
    another operation x6, other arithmetic, per_device(): lower_factor = jnp.linalg.cholesky(gram_total)  33.9 us
    all_to_all x1, blocking collectives, row_sum(): mine = lax.all_to_all(parts, 'row', 0, 0, tiled=False).sum(0)  28 us
    another operation x4, other arithmetic, per_device(): lax.linalg.triangular_solve(lower_factor, totals, left_side=True, lower=T...  20.7 us
    all_to_all x1, waiting for transfers between devices, row_sum(): return lax.all_to_all(copies, 'row', 0, 0, tiled=False).reshape(rows, cols)  8.49 us
    unnamed x9, local copies, waits for them, and re-layouts  5.91 us
    dot_general x1, matrix products, per_device(): lax.dot_general(gathered, gathered, contract_rows, precision=highest)  4.23 us
  transfers between devices with their start and end apart: 2, of which 2 were waited for; matrix products, arithmetic and copies ran while one was open for 1% of the time, Pallas kernels for 0%

commit v1 on v0

--- a/solution.py
+++ b/solution.py
@@ -18,7 +18,21 @@
 
 def per_device(panel, slab):
     highest = lax.Precision.HIGHEST
-    gathered = lax.all_gather(panel, "col", axis=1, tiled=True)
+    ways, here, step = (lax.axis_size("col"), lax.axis_index("col"), panel.shape[1])
+    shape = [n_2 * ways if d == 1 else n_2 for d, n_2 in enumerate(panel.shape)]
+    full = lax.dynamic_update_slice_in_dim(
+        jnp.zeros(shape, panel.dtype), panel, here * step, axis=1
+    )
+    going_up = going_down = panel
+    for far in range(1, ways // 2 + 1):
+        going_up = lax.ppermute(going_up, "col", [(d, (d + 1) % ways) for d in range(ways)])
+        full = lax.dynamic_update_slice_in_dim(full, going_up, (here - far) % ways * step, axis=1)
+        if 2 * far < ways:
+            going_down = lax.ppermute(going_down, "col", [(d, (d - 1) % ways) for d in range(ways)])
+            full = lax.dynamic_update_slice_in_dim(
+                full, going_down, (here + far) % ways * step, axis=1
+            )
+    gathered = full
     cross_local = lax.dot_general(gathered, slab, contract_rows, precision=highest)
     gram_local = lax.dot_general(gathered, gathered, contract_rows, precision=highest)
     width = gram_local.shape[1]

time: 208 us -> 184 us (0.88)
  waiting for transfers between devices: 80.7 us -> 21.3 us
  starting transfers between devices: 3.89 us -> 58.7 us
  between operations: 15.5 us -> 2.77 us
  local copies, waits for them, and re-layouts: 11 us -> 5.75 us
    all_gather x1 -> x0, waiting for transfers between devices: 71.6 us -> none  [per_device(): gathered = lax.all_gather(panel, 'col', axis=1, tiled=True)]
    ppermute x0 -> x15, starting transfers between devices: none -> 54.8 us  [the longest x7 36.9 us: per_device(): lax.ppermute(going_down, 'col', [(d, (d - 1) % ways) for d in range(ways)])]
    ppermute x0 -> x15, waiting for transfers between devices: none -> 9.92 us  [the longest x8 9.9 us: per_device(): lax.ppermute(going_up, 'col', [(d, (d + 1) % ways) for d in range(ways)])]
    unnamed x9 -> x7, local copies, waits for them, and re-layouts: 5.91 us -> 0.15 us
    all_to_all x1, waiting for transfers between devices: 8.49 us -> 11.4 us  [row_sum(): return lax.all_to_all(copies, 'row', 0, 0, tiled=False).reshape(rows, cols)]
    dot_general x1, matrix products: 4.23 us -> 1.86 us  [per_device(): lax.dot_general(gathered, gathered, contract_rows, precision=highest)]
  transfers between devices with their start and end apart: 2 -> 16, of which waited for: 2 -> 9; matrix products, arithmetic and copies ran while one was open for 1% -> 0% of each run, Pallas kernels for 0% -> 0%
where the time goes in v1:
time: 184 us
  starting transfers between devices  58.7 us (32%)
  other arithmetic  55.3 us (30%)
  blocking collectives  27.5 us (15%)
  waiting for transfers between devices  21.3 us (12%)
  matrix products  12.4 us (7%)
  local copies, waits for them, and re-layouts  5.75 us (3%)
  between operations  2.77 us (2%)
    ppermute x7, starting transfers between devices, per_device(): lax.ppermute(going_down, 'col', [(d, (d - 1) % ways) for d in range(ways)])  36.9 us
    another operation x6, other arithmetic, per_device(): lower_factor = jnp.linalg.cholesky(gram_total)  33.9 us
    all_to_all x1, blocking collectives, row_sum(): mine = lax.all_to_all(parts, 'row', 0, 0, tiled=False).sum(0)  27.5 us
    another operation x4, other arithmetic, per_device(): lax.linalg.triangular_solve(lower_factor, totals, left_side=True, lower=T...  20.7 us
    ppermute x8, starting transfers between devices, per_device(): lax.ppermute(going_up, 'col', [(d, (d + 1) % ways) for d in range(ways)])  17.9 us
    all_to_all x1, waiting for transfers between devices, row_sum(): return lax.all_to_all(copies, 'row', 0, 0, tiled=False).reshape(rows, cols)  11.4 us
    ppermute x8, waiting for transfers between devices, per_device(): lax.ppermute(going_up, 'col', [(d, (d + 1) % ways) for d in range(ways)])  9.9 us
    dot_general x1, matrix products, per_device(): residual = slab - jnp.dot(gathered, coefficients, precision=highest)  4.83 us
  transfers between devices with their start and end apart: 16, of which 9 were waited for; matrix products, arithmetic and copies ran while one was open for 0% of the time, Pallas kernels for 0%

profile of v1, /device:TPU:1, one launch (start us, length us, event | category | flops | bytes accessed | tf_op | source)
XLA Modules:
  0.0 183.8 jit_solution(10527016847625688138)
XLA Ops:
  0.6 4.5 %collective-permute-start = (f32[2048,16]{0,1:T(8,128)}, f32[2048,16]{0,1:T(8,128)S(1)}, u32[]{:S(2)}, u32[]{:S(2)}) collective-permute-start(f32[2048,16]{0,1:T(8,128)} %param.2), channel_id=1, source_target_pairs={{0,1},{1,2},{2,3},{3,4},{4,5},{5,6},{6,7},{7,8},{8,9},{9,10},{10,1... | collective-permute-start | bytes 393224 | tf_op jit(solution)/shard_map/ppermute | solution.py:28
  5.2 9.5 %collective-permute-start.1 = (f32[2048,16]{0,1:T(8,128)}, f32[2048,16]{0,1:T(8,128)S(1)}, u32[]{:S(2)}, u32[]{:S(2)}) collective-permute-start(f32[2048,16]{0,1:T(8,128)} %param.2), channel_id=1, source_target_pairs={{0,15},{1,0},{2,1},{3,2},{4,3},{5,4},{6,5},{7,6},{8,7},{9,8},{10,9... | collective-permute-start | bytes 393224 | tf_op jit(solution)/shard_map/ppermute | solution.py:31
  15.2 0.9 collective-permute-done
  16.1 1.9 %collective-permute-start.2 = (f32[2048,16]{0,1:T(8,128)S(1)}, f32[2048,16]{0,1:T(8,128)S(1)}, u32[]{:S(2)}, u32[]{:S(2)}) collective-permute-start(f32[2048,16]{0,1:T(8,128)S(1)} %collective-permute-done), channel_id=1, source_target_pairs={{0,1},{1,2},{2,3},{3,4},{4,5},{5,6},{6,7},{7,8},{8,9},{9,10},{10,1... | collective-permute-start | bytes 393224 | tf_op jit(solution)/shard_map/ppermute | solution.py:28
  18.1 4.6 %collective-permute-start.3 = (f32[2048,16]{0,1:T(8,128)S(1)}, f32[2048,16]{0,1:T(8,128)S(1)}, u32[]{:S(2)}, u32[]{:S(2)}) collective-permute-start(f32[2048,16]{0,1:T(8,128)S(1)} %collective-permute-done.1), channel_id=1, source_target_pairs={{0,15},{1,0},{2,1},{3,2},{4,3},{5,4},{6,5},{7,6},{8,7},{9,8},{10,9... | collective-permute-start | bytes 393224 | tf_op jit(solution)/shard_map/ppermute | solution.py:31
  22.7 0.4 collective-permute-done.2
  23.1 1.9 %collective-permute-start.4 = (f32[2048,16]{0,1:T(8,128)S(1)}, f32[2048,16]{0,1:T(8,128)S(1)}, u32[]{:S(2)}, u32[]{:S(2)}) collective-permute-start(f32[2048,16]{0,1:T(8,128)S(1)} %collective-permute-done.2), channel_id=1, source_target_pairs={{0,1},{1,2},{2,3},{3,4},{4,5},{5,6},{6,7},{7,8},{8,9},{9,10},{10,1... | collective-permute-start | bytes 393224 | tf_op jit(solution)/shard_map/ppermute | solution.py:28
  25.0 4.6 %collective-permute-start.5 = (f32[2048,16]{0,1:T(8,128)S(1)}, f32[2048,16]{0,1:T(8,128)S(1)}, u32[]{:S(2)}, u32[]{:S(2)}) collective-permute-start(f32[2048,16]{0,1:T(8,128)S(1)} %collective-permute-done.3), channel_id=1, source_target_pairs={{0,15},{1,0},{2,1},{3,2},{4,3},{5,4},{6,5},{7,6},{8,7},{9,8},{10,9... | collective-permute-start | bytes 393224 | tf_op jit(solution)/shard_map/ppermute | solution.py:31
  29.6 0.4 collective-permute-done.4
  30.0 1.9 %collective-permute-start.6 = (f32[2048,16]{0,1:T(8,128)S(1)}, f32[2048,16]{0,1:T(8,128)S(1)}, u32[]{:S(2)}, u32[]{:S(2)}) collective-permute-start(f32[2048,16]{0,1:T(8,128)S(1)} %collective-permute-done.4), channel_id=1, source_target_pairs={{0,1},{1,2},{2,3},{3,4},{4,5},{5,6},{6,7},{7,8},{8,9},{9,10},{10,1... | collective-permute-start | bytes 393224 | tf_op jit(solution)/shard_map/ppermute | solution.py:28
  31.9 4.6 %collective-permute-start.7 = (f32[2048,16]{0,1:T(8,128)S(1)}, f32[2048,16]{0,1:T(8,128)S(1)}, u32[]{:S(2)}, u32[]{:S(2)}) collective-permute-start(f32[2048,16]{0,1:T(8,128)S(1)} %collective-permute-done.5), channel_id=1, source_target_pairs={{0,15},{1,0},{2,1},{3,2},{4,3},{5,4},{6,5},{7,6},{8,7},{9,8},{10,9... | collective-permute-start | bytes 393224 | tf_op jit(solution)/shard_map/ppermute | solution.py:31
  36.5 0.4 collective-permute-done.6
  36.9 1.9 %collective-permute-start.8 = (f32[2048,16]{0,1:T(8,128)S(1)}, f32[2048,16]{0,1:T(8,128)S(1)}, u32[]{:S(2)}, u32[]{:S(2)}) collective-permute-start(f32[2048,16]{0,1:T(8,128)S(1)} %collective-permute-done.6), channel_id=1, source_target_pairs={{0,1},{1,2},{2,3},{3,4},{4,5},{5,6},{6,7},{7,8},{8,9},{9,10},{10,1... | collective-permute-start | bytes 393224 | tf_op jit(solution)/shard_map/ppermute | solution.py:28
  38.8 4.6 %collective-permute-start.9 = (f32[2048,16]{0,1:T(8,128)S(1)}, f32[2048,16]{0,1:T(8,128)S(1)}, u32[]{:S(2)}, u32[]{:S(2)}) collective-permute-start(f32[2048,16]{0,1:T(8,128)S(1)} %collective-permute-done.7), channel_id=1, source_target_pairs={{0,15},{1,0},{2,1},{3,2},{4,3},{5,4},{6,5},{7,6},{8,7},{9,8},{10,9... | collective-permute-start | bytes 393224 | tf_op jit(solution)/shard_map/ppermute | solution.py:31
  43.4 0.4 collective-permute-done.8
  43.8 1.9 %collective-permute-start.10 = (f32[2048,16]{0,1:T(8,128)S(1)}, f32[2048,16]{0,1:T(8,128)S(1)}, u32[]{:S(2)}, u32[]{:S(2)}) collective-permute-start(f32[2048,16]{0,1:T(8,128)S(1)} %collective-permute-done.8), channel_id=1, source_target_pairs={{0,1},{1,2},{2,3},{3,4},{4,5},{5,6},{6,7},{7,8},{8,9},{9,10},{10,1... | collective-permute-start | bytes 393224 | tf_op jit(solution)/shard_map/ppermute | solution.py:28
  45.7 4.6 %collective-permute-start.11 = (f32[2048,16]{0,1:T(8,128)S(1)}, f32[2048,16]{0,1:T(8,128)S(1)}, u32[]{:S(2)}, u32[]{:S(2)}) collective-permute-start(f32[2048,16]{0,1:T(8,128)S(1)} %collective-permute-done.9), channel_id=1, source_target_pairs={{0,15},{1,0},{2,1},{3,2},{4,3},{5,4},{6,5},{7,6},{8,7},{9,8},{10,9... | collective-permute-start | bytes 393224 | tf_op jit(solution)/shard_map/ppermute | solution.py:31
  50.4 0.4 collective-permute-done.10
  50.7 1.9 %collective-permute-start.12 = (f32[2048,16]{0,1:T(8,128)S(1)}, f32[2048,16]{0,1:T(8,128)S(1)}, u32[]{:S(2)}, u32[]{:S(2)}) collective-permute-start(f32[2048,16]{0,1:T(8,128)S(1)} %collective-permute-done.10), channel_id=1, source_target_pairs={{0,1},{1,2},{2,3},{3,4},{4,5},{5,6},{6,7},{7,8},{8,9},{9,10},{10,1... | collective-permute-start | bytes 393224 | tf_op jit(solution)/shard_map/ppermute | solution.py:28
  52.6 4.6 %collective-permute-start.13 = (f32[2048,16]{0,1:T(8,128)S(1)}, f32[2048,16]{0,1:T(8,128)S(1)}, u32[]{:S(2)}, u32[]{:S(2)}) collective-permute-start(f32[2048,16]{0,1:T(8,128)S(1)} %collective-permute-done.11), channel_id=1, source_target_pairs={{0,15},{1,0},{2,1},{3,2},{4,3},{5,4},{6,5},{7,6},{8,7},{9,8},{10,9... | collective-permute-start | bytes 393224 | tf_op jit(solution)/shard_map/ppermute | solution.py:31
  57.3 1.1 collective-permute-done.12
  58.4 1.9 %collective-permute-start.14 = (f32[2048,16]{0,1:T(8,128)S(1)}, f32[2048,16]{0,1:T(8,128)S(1)}, u32[]{:S(2)}, u32[]{:S(2)}) collective-permute-start(f32[2048,16]{0,1:T(8,128)S(1)} %collective-permute-done.12), channel_id=1, source_target_pairs={{0,1},{1,2},{2,3},{3,4},{4,5},{5,6},{6,7},{7,8},{8,9},{9,10},{10,1... | collective-permute-start | bytes 393224 | tf_op jit(solution)/shard_map/ppermute | solution.py:28
  60.4 6.1 %collective-permute-done.14 = f32[2048,16]{0,1:T(8,128)S(1)} collective-permute-done((f32[2048,16]{0,1:T(8,128)S(1)}, f32[2048,16]{0,1:T(8,128)S(1)}, u32[]{:S(2)}, u32[]{:S(2)}) %collective-permute-start.14) | collective-permute-done | bytes 131104 | tf_op jit(solution)/shard_map/ppermute | solution.py:28
  66.5 1.9 %fusion.18 = f32[256,256]{0,1:T(8,128)S(1)} fusion(f32[2048,256]{0,1:T(8,128)S(1)} %constant_dynamic-update-slice_fusion.1), kind=kOutput, calls=%fused_computation.58 | convolution fusion | flops 1610612736 | bytes 2359296 | tf_op jit(solution)/shard_map/dot_general | solution.py:37
  68.4 3.6 %fusion.19 = f32[256,256]{0,1:T(8,128)S(1)} fusion(f32[2048,256]{0,1:T(8,128)S(1)} %constant_dynamic-update-slice_fusion.1, f32[2048,256]{1,0:T(8,128)S(1)} %copy-done), kind=kOutput, calls=%fused_computation.59 | convolution fusion | flops 1610612736 | bytes 4456448 | tf_op jit(solution)/shard_map/dot_general | solution.py:36
  72.2 27.5 %all_to_all.10 = f32[32,8,512]{2,1,0:T(8,128)S(1)} all-to-all(f32[32,8,512]{2,1,0:T(8,128)S(1)} %bitcast.49), channel_id=1, replica_groups=mesh['row'=32,'col'=16] {'row'}, dimensions={0} | all-to-all | bytes 1048576 | tf_op jit(solution)/shard_map/all_to_all | solution.py:14
  99.7 0.9 broadcast_in_dim.12
  100.6 3.9 %all-to-all-start.1 = ((f32[32,8,512]{2,1,0:T(8,128)}), f32[32,8,512]{2,1,0:T(8,128)S(1)}, u32[]{:S(2)}, u32[]{:S(2)}) async-start(f32[32,8,512]{2,1,0:T(8,128)} %broadcast_in_dim.12), calls=%async_computation.1 | async-start | bytes 1048576 | tf_op jit(solution)/shard_map/all_to_all | solution.py:16
  104.5 11.4 %all-to-all-done.1 = f32[32,8,512]{2,1,0:T(8,128)S(1)} async-done(((f32[32,8,512]{2,1,0:T(8,128)}), f32[32,8,512]{2,1,0:T(8,128)S(1)}, u32[]{:S(2)}, u32[]{:S(2)}) %all-to-all-start.1) | async-done | bytes 524320 | tf_op jit(solution)/shard_map/all_to_all | solution.py:16
  116.1 11.7 %cholesky.50 = f32[128,128]{1,0:T(8,128)S(1)} custom-call(f32[128,128]{1,0:T(8,128)S(1)} %cholesky.118), custom_call_target="Cholesky" | custom-call | tf_op jit(solution)/shard_map/jit(cholesky)/cholesky | solution.py:41
  127.8 9.8 %custom-call.16 = f32[1,128,128]{1,2,0:T(8,128)S(1)} custom-call(f32[1,128,128]{2,1,0:T(8,128)S(1)} %get-tuple-element.26), custom_call_target="InvertDiagBlocksLowerTriangular" | custom-call | tf_op jit(solution)/shard_map/jit(cholesky)/cholesky | solution.py:41
  137.9 0.3 convolution_subtract_fusion.3
  138.1 11.7 %cholesky.105 = f32[128,128]{1,0:T(8,128)S(1)} custom-call(f32[128,128]{1,0:T(8,128)S(1)} %convolution_subtract_fusion.3), custom_call_target="Cholesky" | custom-call | tf_op jit(solution)/shard_map/jit(cholesky)/cholesky | solution.py:41
  149.9 0.6 compare_reduce_fusion
  152.0 4.0 %while.1 = (s32[]{:T(128)}, f32[256,256]{1,0:T(8,128)S(1)}, s32[2,2]{1,0:T(2,128)S(1)}, f32[2,128,128]{2,1,0:T(8,128)S(1)}, s32[]{:T(128)}) while((s32[]{:T(128)}, f32[256,256]{1,0:T(8,128)S(1)}, s32[2,2]{1,0:T(2,128)S(1)}, f32[2,128,128]{2,1,0:T(8,128)S(1)}, s32[]{:T(128)}) %tuple.28), condition=%wide.while_cond, body=%wide.while_body.sunk | while | flops 2 | bytes 131189 | solution.py:42
  152.0 0.6 fusion.33
  152.5 1.4 bitcast_dynamic-update-slice_fusion.2
  154.0 0.6 fusion.33
  154.5 1.4 bitcast_dynamic-update-slice_fusion.2
  155.9 19.9 %custom-call.17 = f32[2,128,128]{1,2,0:T(8,128)S(1)} custom-call(f32[2,128,128]{2,1,0:T(8,128)S(1)} %get-tuple-element.10), custom_call_target="InvertDiagBlocksLowerTriangular" | custom-call | tf_op jit(solution)/shard_map/triangular_solve | solution.py:42
  175.9 0.3 fusion.5
  176.2 0.3 convolution_subtract_fusion.2
  176.4 0.3 fusion.12
  176.8 0.7 pad_maximum_fusion.1
  177.8 0.6 fusion.15
  178.4 0.3 convolution_subtract_fusion.1
  178.7 0.3 fusion.10
  179.0 4.8 %convolution_subtract_fusion = f32[2048,256]{1,0:T(8,128)} fusion(f32[2048,256]{1,0:T(8,128)S(1)} %copy-done.1, f32[2048,256]{0,1:T(8,128)S(1)} %constant_dynamic-update-slice_fusion.1, f32[128,256]{1,0:T(8,128)S(1)} %fusion.11, f32[128,256]{1,0:T(8,128)S(1)} %fusion.10), kind=kOutput, calls=%fused_computation.2 | convolution fusion | flops 1611202560 | bytes 6553600 | tf_op jit(solution)/shard_map/dot_general | solution.py:48
  (48 shorter events, 1.7 us)
Async XLA Ops:
  0.6 14.6 %copy-start.2 = (f32[2048,16]{0,1:T(8,128)S(1)}, f32[2048,16]{0,1:T(8,128)}, u32[]{:S(2)}) copy-start(f32[2048,16]{0,1:T(8,128)} %param.2) | copy-start | bytes 393220
  0.6 15.5 %collective-permute-start = (f32[2048,16]{0,1:T(8,128)}, f32[2048,16]{0,1:T(8,128)S(1)}, u32[]{:S(2)}, u32[]{:S(2)}) collective-permute-start(f32[2048,16]{0,1:T(8,128)} %param.2), channel_id=1, source_target_pairs={{0,1},{1,2},{2,3},{3,4},{4,5},{5,6},{6,7},{7,8},{8,9},{9,10},{10,1... | collective-permute-start | bytes 393224 | tf_op jit(solution)/shard_map/ppermute | solution.py:28
  5.2 12.9 %collective-permute-start.1 = (f32[2048,16]{0,1:T(8,128)}, f32[2048,16]{0,1:T(8,128)S(1)}, u32[]{:S(2)}, u32[]{:S(2)}) collective-permute-start(f32[2048,16]{0,1:T(8,128)} %param.2), channel_id=1, source_target_pairs={{0,15},{1,0},{2,1},{3,2},{4,3},{5,4},{6,5},{7,6},{8,7},{9,8},{10,9... | collective-permute-start | bytes 393224 | tf_op jit(solution)/shard_map/ppermute | solution.py:31
  16.1 6.9 %collective-permute-start.2 = (f32[2048,16]{0,1:T(8,128)S(1)}, f32[2048,16]{0,1:T(8,128)S(1)}, u32[]{:S(2)}, u32[]{:S(2)}) collective-permute-start(f32[2048,16]{0,1:T(8,128)S(1)} %collective-permute-done), channel_id=1, source_target_pairs={{0,1},{1,2},{2,3},{3,4},{4,5},{5,6},{6,7},{7,8},{8,9},{9,10},{10,1... | collective-permute-start | bytes 393224 | tf_op jit(solution)/shard_map/ppermute | solution.py:28
  18.1 6.9 %collective-permute-start.3 = (f32[2048,16]{0,1:T(8,128)S(1)}, f32[2048,16]{0,1:T(8,128)S(1)}, u32[]{:S(2)}, u32[]{:S(2)}) collective-permute-start(f32[2048,16]{0,1:T(8,128)S(1)} %collective-permute-done.1), channel_id=1, source_target_pairs={{0,15},{1,0},{2,1},{3,2},{4,3},{5,4},{6,5},{7,6},{8,7},{9,8},{10,9... | collective-permute-start | bytes 393224 | tf_op jit(solution)/shard_map/ppermute | solution.py:31
  23.1 6.9 %collective-permute-start.4 = (f32[2048,16]{0,1:T(8,128)S(1)}, f32[2048,16]{0,1:T(8,128)S(1)}, u32[]{:S(2)}, u32[]{:S(2)}) collective-permute-start(f32[2048,16]{0,1:T(8,128)S(1)} %collective-permute-done.2), channel_id=1, source_target_pairs={{0,1},{1,2},{2,3},{3,4},{4,5},{5,6},{6,7},{7,8},{8,9},{9,10},{10,1... | collective-permute-start | bytes 393224 | tf_op jit(solution)/shard_map/ppermute | solution.py:28
  25.0 6.9 %collective-permute-start.5 = (f32[2048,16]{0,1:T(8,128)S(1)}, f32[2048,16]{0,1:T(8,128)S(1)}, u32[]{:S(2)}, u32[]{:S(2)}) collective-permute-start(f32[2048,16]{0,1:T(8,128)S(1)} %collective-permute-done.3), channel_id=1, source_target_pairs={{0,15},{1,0},{2,1},{3,2},{4,3},{5,4},{6,5},{7,6},{8,7},{9,8},{10,9... | collective-permute-start | bytes 393224 | tf_op jit(solution)/shard_map/ppermute | solution.py:31
  30.0 6.9 %collective-permute-start.6 = (f32[2048,16]{0,1:T(8,128)S(1)}, f32[2048,16]{0,1:T(8,128)S(1)}, u32[]{:S(2)}, u32[]{:S(2)}) collective-permute-start(f32[2048,16]{0,1:T(8,128)S(1)} %collective-permute-done.4), channel_id=1, source_target_pairs={{0,1},{1,2},{2,3},{3,4},{4,5},{5,6},{6,7},{7,8},{8,9},{9,10},{10,1... | collective-permute-start | bytes 393224 | tf_op jit(solution)/shard_map/ppermute | solution.py:28
  31.9 6.9 %collective-permute-start.7 = (f32[2048,16]{0,1:T(8,128)S(1)}, f32[2048,16]{0,1:T(8,128)S(1)}, u32[]{:S(2)}, u32[]{:S(2)}) collective-permute-start(f32[2048,16]{0,1:T(8,128)S(1)} %collective-permute-done.5), channel_id=1, source_target_pairs={{0,15},{1,0},{2,1},{3,2},{4,3},{5,4},{6,5},{7,6},{8,7},{9,8},{10,9... | collective-permute-start | bytes 393224 | tf_op jit(solution)/shard_map/ppermute | solution.py:31
  36.9 6.9 %collective-permute-start.8 = (f32[2048,16]{0,1:T(8,128)S(1)}, f32[2048,16]{0,1:T(8,128)S(1)}, u32[]{:S(2)}, u32[]{:S(2)}) collective-permute-start(f32[2048,16]{0,1:T(8,128)S(1)} %collective-permute-done.6), channel_id=1, source_target_pairs={{0,1},{1,2},{2,3},{3,4},{4,5},{5,6},{6,7},{7,8},{8,9},{9,10},{10,1... | collective-permute-start | bytes 393224 | tf_op jit(solution)/shard_map/ppermute | solution.py:28
  38.8 6.9 %collective-permute-start.9 = (f32[2048,16]{0,1:T(8,128)S(1)}, f32[2048,16]{0,1:T(8,128)S(1)}, u32[]{:S(2)}, u32[]{:S(2)}) collective-permute-start(f32[2048,16]{0,1:T(8,128)S(1)} %collective-permute-done.7), channel_id=1, source_target_pairs={{0,15},{1,0},{2,1},{3,2},{4,3},{5,4},{6,5},{7,6},{8,7},{9,8},{10,9... | collective-permute-start | bytes 393224 | tf_op jit(solution)/shard_map/ppermute | solution.py:31
  43.8 6.9 %collective-permute-start.10 = (f32[2048,16]{0,1:T(8,128)S(1)}, f32[2048,16]{0,1:T(8,128)S(1)}, u32[]{:S(2)}, u32[]{:S(2)}) collective-permute-start(f32[2048,16]{0,1:T(8,128)S(1)} %collective-permute-done.8), channel_id=1, source_target_pairs={{0,1},{1,2},{2,3},{3,4},{4,5},{5,6},{6,7},{7,8},{8,9},{9,10},{10,1... | collective-permute-start | bytes 393224 | tf_op jit(solution)/shard_map/ppermute | solution.py:28
  45.7 6.9 %collective-permute-start.11 = (f32[2048,16]{0,1:T(8,128)S(1)}, f32[2048,16]{0,1:T(8,128)S(1)}, u32[]{:S(2)}, u32[]{:S(2)}) collective-permute-start(f32[2048,16]{0,1:T(8,128)S(1)} %collective-permute-done.9), channel_id=1, source_target_pairs={{0,15},{1,0},{2,1},{3,2},{4,3},{5,4},{6,5},{7,6},{8,7},{9,8},{10,9... | collective-permute-start | bytes 393224 | tf_op jit(solution)/shard_map/ppermute | solution.py:31
  50.7 7.7 %collective-permute-start.12 = (f32[2048,16]{0,1:T(8,128)S(1)}, f32[2048,16]{0,1:T(8,128)S(1)}, u32[]{:S(2)}, u32[]{:S(2)}) collective-permute-start(f32[2048,16]{0,1:T(8,128)S(1)} %collective-permute-done.10), channel_id=1, source_target_pairs={{0,1},{1,2},{2,3},{3,4},{4,5},{5,6},{6,7},{7,8},{8,9},{9,10},{10,1... | collective-permute-start | bytes 393224 | tf_op jit(solution)/shard_map/ppermute | solution.py:28
  52.6 7.7 %collective-permute-start.13 = (f32[2048,16]{0,1:T(8,128)S(1)}, f32[2048,16]{0,1:T(8,128)S(1)}, u32[]{:S(2)}, u32[]{:S(2)}) collective-permute-start(f32[2048,16]{0,1:T(8,128)S(1)} %collective-permute-done.11), channel_id=1, source_target_pairs={{0,15},{1,0},{2,1},{3,2},{4,3},{5,4},{6,5},{7,6},{8,7},{9,8},{10,9... | collective-permute-start | bytes 393224 | tf_op jit(solution)/shard_map/ppermute | solution.py:31
  58.4 8.1 %collective-permute-start.14 = (f32[2048,16]{0,1:T(8,128)S(1)}, f32[2048,16]{0,1:T(8,128)S(1)}, u32[]{:S(2)}, u32[]{:S(2)}) collective-permute-start(f32[2048,16]{0,1:T(8,128)S(1)} %collective-permute-done.12), channel_id=1, source_target_pairs={{0,1},{1,2},{2,3},{3,4},{4,5},{5,6},{6,7},{7,8},{8,9},{9,10},{10,1... | collective-permute-start | bytes 393224 | tf_op jit(solution)/shard_map/ppermute | solution.py:28
  66.5 1.9 %copy-start = (f32[2048,256]{1,0:T(8,128)S(1)}, f32[2048,256]{1,0:T(8,128)}, u32[]{:S(2)}) copy-start(f32[2048,256]{1,0:T(8,128)} %param.3) | copy-start | bytes 6291460
  100.6 15.3 %all-to-all-start.1 = ((f32[32,8,512]{2,1,0:T(8,128)}), f32[32,8,512]{2,1,0:T(8,128)S(1)}, u32[]{:S(2)}, u32[]{:S(2)}) async-start(f32[32,8,512]{2,1,0:T(8,128)} %broadcast_in_dim.12), calls=%async_computation.1 | async-start | bytes 1048576 | tf_op jit(solution)/shard_map/all_to_all | solution.py:16
  175.8 3.1 %copy-start.1 = (f32[2048,256]{1,0:T(8,128)S(1)}, f32[2048,256]{1,0:T(8,128)}, u32[]{:S(2)}) copy-start(f32[2048,256]{1,0:T(8,128)} %param.3) | copy-start | bytes 6291460
